TPU v7x, 32 devices: a whole 2x2x4 slice. The times are simulated.
32 devices in a mesh: groups: 2 (over y), seq: 4 (over z), tensor: 4 (over x, core).
Axes of the slice: x: 2, y: 2, z: 4, core: 2. Of those that a mesh axis runs over, the one named last changes fastest.
Arguments:
- x_in: bfloat16 [4096, 5120], P(('groups', 'seq'), 'tensor'), parts along dimension 0, may hold values from -6 to 6
- z_gate: bfloat16 [4096, 5120], P(('groups', 'seq'), 'tensor'), parts along dimension 0, may hold values from -32 to 32
- bc_in: bfloat16 [4096, 256], P(('groups', 'seq')), parts along dimension 0, may hold values from -6 to 6
- step_size: float32 [80, 4096], P('tensor', ('groups', 'seq')), parts along dimension 1, may hold values from 0 to 0.4
- log_keep: float32 [80, 4096], P('tensor', ('groups', 'seq')), parts along dimension 1, may hold values from -1 to 0
- skip_gain: float32 [80], P('tensor'), may hold values from 0.5 to 2
- conv_x: bfloat16 [4, 5120], P(None, 'tensor'), may hold values from -3 to 3
- conv_bc: bfloat16 [4, 256], replicated, may hold values from -3 to 3
- norm_gain: float32 [5120], P('tensor'), may hold values from 0.1 to 1.9
- seg_ends: int32 [1024], P(('groups', 'seq')), parts along dimension 0, may hold values from 0 to 2047, as said below
- pool_query: bfloat16 [320, 5120], P(('groups', 'seq'), 'tensor'), parts along dimension 0, may hold values from -64 to 64
- pool_start: int32 [320], P(('groups', 'seq')), parts along dimension 0, may hold values from 0 to 255, as said below
- pool_stop: int32 [320], P(('groups', 'seq')), parts along dimension 0, may hold values from 64 to 512
Outputs:
- mixed_seq: bfloat16 [4096, 5120], P(('groups', 'seq'), 'tensor'), parts along dimension 0
- pooled: float32 [320, 5120], P(('groups', 'seq'), 'tensor'), parts along dimension 0
There are 2 independent parts, one for each index of `groups`. A program takes and returns all parts, laid end to end along the dimension named above; an argument that names none is the same for every part. Nothing has to cross between parts.
Inputs may be any that keep to these rules, and one draw needn't show every extreme that they name: The tokens fall into blocks of 512; block b holds exactly the 128 segment ends seg_ends[b * 128] to seg_ends[(b + 1) * 128 - 1], strictly increasing. pool_start < pool_stop for every pooled row.
All inputs are finite; a program needn't handle non-finite values.
Results may differ from a plain program's by a relative error of at most 0.039.
Values may be sent and summed in bfloat16 or wider, within the bound.
No kernel may reach another device: no remote copies, remote signals or barrier semaphores. Data moves between devices by JAX's collectives and lax.ppermute only.
A program may use at most 64 MiB of HBM per device.

v0:
```python
import math
import jax
import jax.numpy as jnp
from jax import lax
from jax.sharding import PartitionSpec as P

STRETCH = 256
POOL_HEADS = 32
EPSILON = 1e-05
MASKED = -1e30


def passed_along(value, axis, steps):
    count = lax.axis_size(axis)
    leading, last = (max(0, -steps), min(count, count - steps))
    return lax.ppermute(value, axis, [(source, source + steps) for source in range(leading, last)])


def prefix(part, axis, combine, identity):
    place = lax.axis_index(axis)
    gathered = jax.tree.map(lambda a: lax.all_gather(a, axis), part)
    state = jax.tree.map(lambda a, e: jnp.zeros_like(a) + jnp.asarray(e, a.dtype), part, identity)

    def one(lap, state):
        return combine(
            state, jax.tree.map(lambda a: lax.dynamic_index_in_dim(a, lap, 0, False), gathered)
        )

    return lax.fori_loop(0, place, one, state)


def silu_act(values):
    return values / (1.0 + jnp.exp(-values))


def causal_conv(before, current, weights):
    kernel_width = weights.shape[0]
    length = current.shape[0]
    padded = jnp.concatenate([before, current], axis=0)
    summed = jnp.zeros(current.shape, jnp.float32)
    for offset in range(kernel_width):
        summed = summed + padded[offset : offset + length].astype(jnp.float32) * weights[
            offset
        ].astype(jnp.float32)
    return silu_act(summed).astype(jnp.bfloat16)


def stretch_local(x_block, b_block, c_block, step_block, keep_block):
    block_len = x_block.shape[0]
    cumul_keep = jnp.cumsum(keep_block, axis=1)
    lower_mask = lax.broadcasted_iota(jnp.int32, (block_len, block_len), 0) >= lax.broadcasted_iota(
        jnp.int32, (block_len, block_len), 1
    )
    inner_prod = jnp.einsum("is,js->ij", c_block, b_block, preferred_element_type=jnp.float32)
    spread = cumul_keep[:, :, None] - cumul_keep[:, None, :]
    decay_mask = jnp.where(lower_mask[None], jnp.exp(jnp.where(lower_mask[None], spread, 0.0)), 0.0)
    mixing = (decay_mask * inner_prod[None] * step_block[:, None, :]).astype(jnp.bfloat16)
    intra_part = jnp.einsum("hij,jhp->ihp", mixing, x_block, preferred_element_type=jnp.float32)
    tail_weight = jnp.exp(cumul_keep[:, -1:] - cumul_keep) * step_block
    weighted = (tail_weight.T[:, :, None] * x_block.astype(jnp.float32)).astype(jnp.bfloat16)
    stretch_state = jnp.einsum("jhp,js->hps", weighted, b_block, preferred_element_type=jnp.float32)
    return (intra_part, stretch_state, cumul_keep)


def combine(earlier, later):
    return (earlier[0] * jnp.exp(later[1])[:, None, None] + later[0], earlier[1] + later[1])


def read_state(c_block, state_in):
    state_high = state_in.astype(jnp.bfloat16)
    state_low = (state_in - state_high.astype(jnp.float32)).astype(jnp.bfloat16)
    high_part = jnp.einsum("is,hps->ihp", c_block, state_high, preferred_element_type=jnp.float32)
    low_part = jnp.einsum("is,hps->ihp", c_block, state_low, preferred_element_type=jnp.float32)
    return high_part + low_part


def local(
    x_in,
    z_gate,
    bc_in,
    step_size,
    log_keep,
    skip_gain,
    conv_x,
    conv_bc,
    norm_gain,
    seg_ends,
    pool_query,
    pool_start,
    pool_stop,
):
    tok_rows = x_in.shape[0]
    channels = x_in.shape[1]
    heads_local = step_size.shape[0]
    head_width = channels // heads_local
    state_width = bc_in.shape[1] // 2
    rim_rows = conv_x.shape[0] - 1
    edge_rows = jnp.concatenate([x_in[tok_rows - rim_rows :], bc_in[tok_rows - rim_rows :]], axis=1)
    before = passed_along(edge_rows, "seq", 1)
    x_conv = causal_conv(before[:, :channels], x_in, conv_x)
    bc_conv = causal_conv(before[:, channels:], bc_in, conv_bc)
    b_mat = bc_conv[:, :state_width]
    c_mat = bc_conv[:, state_width:]
    x_heads = x_conv.reshape(tok_rows, heads_local, head_width)
    stretch_count = tok_rows // STRETCH
    entry_state = jnp.zeros((heads_local, head_width, state_width), jnp.float32)
    decay_total = jnp.zeros((heads_local,), jnp.float32)
    saved_parts = []
    for block_index in range(stretch_count):
        first_row = block_index * STRETCH
        last_row = first_row + STRETCH
        intra_part, stretch_state, cumul_keep = stretch_local(
            x_heads[first_row:last_row],
            b_mat[first_row:last_row],
            c_mat[first_row:last_row],
            step_size[:, first_row:last_row],
            log_keep[:, first_row:last_row],
        )
        saved_parts.append((intra_part, cumul_keep, entry_state, decay_total))
        entry_state = jnp.exp(cumul_keep[:, -1])[:, None, None] * entry_state + stretch_state
        decay_total = decay_total + cumul_keep[:, -1]
    incoming, unused = prefix(
        (entry_state, decay_total),
        "seq",
        combine,
        (jnp.zeros_like(entry_state), jnp.zeros_like(decay_total)),
    )
    pieces_out = []
    for block_index in range(stretch_count):
        intra_part, cumul_keep, entry_part, decay_part = saved_parts[block_index]
        first_row = block_index * STRETCH
        state_in = entry_part + jnp.exp(decay_part)[:, None, None] * incoming
        from_state = read_state(c_mat[first_row : first_row + STRETCH], state_in)
        pieces_out.append(intra_part + jnp.exp(cumul_keep).T[:, :, None] * from_state)
    ssd_out = jnp.concatenate(pieces_out, axis=0) + skip_gain[None, :, None] * x_heads.astype(
        jnp.float32
    )
    gated = ssd_out.reshape(tok_rows, channels) * silu_act(z_gate.astype(jnp.float32))
    square_sum = lax.psum(jnp.sum(gated * gated, axis=1), "tensor")
    width_all = channels * lax.axis_size("tensor")
    mixed_seq = (
        gated * lax.rsqrt(square_sum / width_all + EPSILON)[:, None] * norm_gain[None, :]
    ).astype(jnp.bfloat16)
    local_ends = seg_ends - lax.axis_index("seq") * tok_rows
    summaries = jnp.take(mixed_seq, local_ends, axis=0)
    pool_heads_local = POOL_HEADS // lax.axis_size("tensor")
    pool_width = channels // pool_heads_local
    scale_factor = 1.0 / math.sqrt(pool_width)
    pools_local = pool_query.shape[0]
    queries = pool_query.reshape(pools_local, pool_heads_local, pool_width)
    piece = lax.all_gather(summaries, "seq", axis=0, tiled=True)
    peak = jnp.full((pool_heads_local, pools_local), MASKED, jnp.float32)
    numer = jnp.zeros((pools_local, pool_heads_local, pool_width), jnp.float32)
    count = piece.shape[0]
    seg_index = lax.iota(jnp.int32, count)
    inside = (seg_index[None, :] >= pool_start[:, None]) & (seg_index[None, :] < pool_stop[:, None])
    keys_block = piece.reshape(count, pool_heads_local, pool_width)
    logits = (
        jnp.einsum("pad,rad->apr", queries, keys_block, preferred_element_type=jnp.float32)
        * scale_factor
    )
    logits = jnp.where(inside[None], logits, MASKED)
    new_peak = jnp.maximum(peak, jnp.max(logits, axis=2))
    expo = jnp.where(inside[None], jnp.exp(logits - new_peak[:, :, None]), 0.0)
    rescale = jnp.exp(peak - new_peak)
    denom = jnp.sum(expo, axis=2)
    numer = numer * rescale.T[:, :, None] + jnp.einsum(
        "apr,rad->pad", expo.astype(jnp.bfloat16), keys_block, preferred_element_type=jnp.float32
    )
    peak, denom, numer = (new_peak, denom, numer)
    pooled = (numer / denom.T[:, :, None]).reshape(pools_local, channels)
    return (mixed_seq, pooled)


def solution(mesh):
    in_specs = (
        P(("groups", "seq"), "tensor"),
        P(("groups", "seq"), "tensor"),
        P(("groups", "seq"), None),
        P("tensor", ("groups", "seq")),
        P("tensor", ("groups", "seq")),
        P("tensor"),
        P(None, "tensor"),
        P(),
        P("tensor"),
        P(("groups", "seq")),
        P(("groups", "seq"), "tensor"),
        P(("groups", "seq")),
        P(("groups", "seq")),
    )
    out_specs = (P(("groups", "seq"), "tensor"), P(("groups", "seq"), "tensor"))
    return jax.shard_map(local, mesh=mesh, in_specs=in_specs, out_specs=out_specs, check_vma=False)
```

profile of v0, /device:TPU:0, one launch (start us, length us, event | category | flops | bytes accessed | tf_op | source)
XLA Modules:
  0.0 157.4 jit_solution(5044019205403970520)
XLA Ops:
  7.2 0.0 all-gather.7.cloned.1.call-start
  7.2 0.7 slice.120
  7.9 0.7 slice.121
  8.7 5.0 %collective-permute-start = (bf16[3,1536]{1,0:T(4,128)(2,1)S(1)}, bf16[3,1536]{1,0:T(4,128)(2,1)S(1)}, u32[]{:S(2)}, u32[]{:S(2)}) collective-permute-start(bf16[3,1536]{1,0:T(4,128)(2,1)S(1)} %pad_maximum_fusion.2), channel_id=1, source_target_pairs={{0,4},{4,8},{8,12},{1,5},{5,9},{9,13},{2,6},{6,10},{10,14},{3,7},{... | collective-permute-start | bytes 27656 | tf_op jit(solution)/shard_map/ppermute | solution.py:16
  13.6 0.8 fusion.71
  14.4 0.6 reduce-window.14
  15.0 0.2 slice_reduce_fusion.1
  15.2 0.1 broadcast_add_fusion.1
  15.4 0.6 reduce-window.16
  16.0 0.2 slice_reduce_fusion
  16.2 0.1 broadcast_add_fusion
  16.3 0.8 slice_convert_fusion.3
  17.2 0.8 slice_reduce_fusion.2
  17.9 0.5 fusion.72
  18.5 1.5 fusion.70
  19.9 0.9 convert_reduce_fusion.3
  20.8 0.6 exp.65
  21.5 4.0 %divide_convert_fusion = bf16[512,1280]{1,0:T(8,128)(2,1)S(1)} fusion(bf16[512,1280]{1,0:T(8,128)(2,1)} %param.15, bf16[3,1280]{1,0:T(4,128)(2,1)S(1)} %slice.158, f32[1280]{0:T(1024)S(1)} %get-tuple-element.52, f32[1280]{0:T(1024)S(1)} %get-tuple-element.53, f32[1280]{0:T(1024)S(1)} %get-tuple-element.51, f32[1280]{0:T(1024)S(1)} %get-tuple-element.50), kind=kLoop, calls=%fused_computation.25 | loop fusion | flops 15728640 | bytes 2649600 | tf_op jit(solution)/shard_map/convert_element_type | solution.py:45
  25.5 0.1 fusion.69
  25.6 0.2 copy.34
  25.8 0.2 copy.39
  26.1 1.9 %divide_convert_fusion.1 = bf16[512,256]{1,0:T(8,128)(2,1)S(1)} fusion(bf16[512,256]{1,0:T(8,128)(2,1)} %param.17, bf16[3,256]{1,0:T(4,128)(2,1)S(1)} %slice.165, f32[256]{0:T(256)S(1)} %bitcast.90, f32[256]{0:T(256)S(1)} %bitcast.91, f32[256]{0:T(256)S(1)} %bitcast.89, f32[256]{0:T(256)S(1)} %bitcast.88), kind=kLoop, calls=%fused_computation.59 | loop fusion | flops 3145728 | bytes 529920 | tf_op jit(solution)/shard_map/convert_element_type | solution.py:45
  28.0 1.1 convolution_add_fusion.3
  29.1 1.9 %convolution_add_fusion.2 = f32[20,64,128]{2,1,0:T(8,128)} fusion(bf16[256,20,64]{0,2,1:T(8,128)(2,1)S(1)} %bitcast.75, f32[256,20]{0,1:T(8,128)} %get-tuple-element.72, f32[20,64,128]{2,1,0:T(8,128)S(1)} %convolution_add_fusion.3, f32[20]{0:T(128)} %exp.65, bf16[512,256]{1,0:T(8,128)(2,1)S(1)} %divide_convert_fusion.1), kind=kOutput, calls=%fused_computation.43 | convolution fusion | flops 85196800 | bytes 2052176 | tf_op jit(solution)/shard_map/jhp,js->hps/dot_general | solution.py:61
  31.0 0.0 all-gather.7.cloned.1.call-update
  31.0 0.0 all-gather.5.cloned.1.call-start
  31.1 1.2 dynamic-slice
  33.0 0.9 dynamic-update-slice
  33.8 10.1 %all-reduce = f32[80]{0:T(128)S(1)} all-reduce(f32[80]{0:T(128)S(1)} %dynamic-update-slice), channel_id=2, replica_groups=mesh['groups'=2,'seq'=4,'tensor'=4] {'seq'}, use_global_device_ids=true, to_apply=%add | all-reduce | flops 80 | bytes 640
  44.0 0.1 reshape.210
  44.1 0.7 mul.319
  44.8 0.7 mul.320
  45.4 0.7 compare_and_fusion
  46.2 0.2 fusion.57
  46.3 0.2 fusion.53
  46.5 3.7 %fusion.18 = f32[256,20,64]{0,2,1:T(8,128)} fusion(bf16[256,20,64]{0,2,1:T(8,128)(2,1)S(1)} %bitcast.78, f32[20,256]{1,0:T(8,128)} %get-tuple-element.70, f32[256,256]{1,0:T(8,128)S(1)} %fusion.57, f32[20,256]{1,0:T(8,128)} %bitcast.81, pred[256,256]{1,0:T(8,128)(4,1)S(1)} %iota_compare_fusion), kind=kOutput, calls=%fused_computation.31 | convolution fusion | flops 175636480 | bytes 2334720 | tf_op jit(solution)/shard_map/hij,jhp->ihp/dot_general | solution.py:58
  50.3 2.9 %fusion.17 = f32[256,20,64]{0,2,1:T(8,128)} fusion(bf16[256,20,64]{0,2,1:T(8,128)(2,1)S(1)} %bitcast.76, f32[20,256]{1,0:T(8,128)S(1)} %copy-done.11, f32[256,256]{1,0:T(8,128)S(1)} %fusion.53, f32[20,256]{1,0:T(8,128)S(1)} %bitcast.84, pred[256,256]{1,0:T(8,128)(4,1)S(1)} %iota_compare_fusion), kind=kOutput, calls=%fused_computation.30 | convolution fusion | flops 175636480 | bytes 2334720 | tf_op jit(solution)/shard_map/hij,jhp->ihp/dot_general | solution.py:58
  53.1 33.0 %all-gather.7.cloned.1.call-done = f32[80,64,128]{2,1,0:T(8,128)} async-done(((f32[20,64,128]{2,1,0:T(8,128)}), f32[80,64,128]{2,1,0:T(8,128)}) %all-gather.7.cloned.1.call-update) | async-done | bytes 2621456 | tf_op jit(solution)/shard_map/all_gather | solution.py:21
  86.2 0.1 broadcast.82
  86.3 0.3 fusion.44
  86.6 0.4 copy-done.9
  87.0 0.6 copy-done.3
  87.6 1.4 fusion.21
  89.0 2.8 %copy.40 = f32[256,1280]{1,0:T(8,128)} copy(f32[256,1280]{0,1:T(8,128)} %bitcast.73) | data formatting | bytes 2621440 | tf_op jit(solution)/shard_map/concatenate | solution.py:135
  91.8 0.4 fusion.41
  92.2 0.9 copy-done.2
  93.1 1.4 fusion.22
  94.6 2.9 %copy.41 = f32[256,1280]{1,0:T(8,128)} copy(f32[256,1280]{0,1:T(8,128)} %bitcast.72) | data formatting | bytes 2621440 | tf_op jit(solution)/shard_map/concatenate | solution.py:135
  97.5 4.2 %multiply_reduce_fusion = (f32[512]{0:T(512)S(1)}, f32[512,1280]{1,0:T(8,128)}) fusion(bf16[512,1280]{1,0:T(8,128)(2,1)} %param.16, bf16[512,1280]{1,0:T(8,128)(2,1)S(1)} %divide_convert_fusion, f32[1280]{0:T(1024)S(1)} %copy-done.10, f32[256,1280]{1,0:T(8,128)} %copy.41, f32[256,1280]{1,0:T(8,128)S(1)} %copy-done.1), kind=kLoop, calls=%fused_computation.14 | loop fusion | flops 7208448 | bytes 7871488 | tf_op jit(solution)/shard_map/reduce_sum | solution.py:139
  101.7 6.4 %psum.7 = f32[512]{0:T(512)S(1)} all-reduce(f32[512]{0:T(512)S(1)} %get-tuple-element.66), channel_id=1, replica_groups=mesh['groups'=2,'seq'=4,'tensor'=4] {'tensor'}, use_global_device_ids=true, to_apply=%region_7.8 | all-reduce | flops 512 | bytes 4096 | tf_op jit(solution)/shard_map/psum | solution.py:139
  108.1 2.0 %multiply_convert_fusion.4 = bf16[512,1280]{1,0:T(8,128)(2,1)S(1)} fusion(f32[512,1280]{1,0:T(8,128)} %get-tuple-element.67, f32[1280]{0:T(1024)S(1)} %copy-done.12, f32[512]{0:T(512)S(1)} %add_rsqrt_fusion), kind=kLoop, calls=%fused_computation.13 | loop fusion | flops 1966080 | bytes 3939328 | tf_op jit(solution)/shard_map/convert_element_type | solution.py:143
  110.1 0.0 copy-start
  110.2 0.9 gather_fusion
  111.1 0.8 broadcast_select_fusion
  111.9 0.0 all-gather.5.cloned.1.call-update
  112.0 0.2 reshape.192
  112.2 0.1 fusion.46
  112.3 34.4 %all-gather.5.cloned.1.call-done = bf16[512,1280]{1,0:T(8,128)(2,1)} async-done(((bf16[128,1280]{1,0:T(8,128)(2,1)}), bf16[512,1280]{1,0:T(8,128)(2,1)}) %all-gather.5.cloned.1.call-update) | async-done | bytes 1310736 | tf_op jit(solution)/shard_map/all_gather | solution.py:151
  146.7 1.6 %copy.42 = bf16[512,1280]{0,1:T(8,128)(2,1)S(1)} copy(bf16[512,1280]{1,0:T(8,128)(2,1)} %all-gather.5.cloned.1.call-done) | data formatting | bytes 2621440 | tf_op jit(solution)/shard_map/all_gather | solution.py:151
  148.3 0.4 fusion.73
  148.7 0.3 fusion.31
  149.0 0.6 fusion.28
  149.6 0.1 copy.44
  149.7 0.8 reshape.193
  (52 shorter events, 0.4 us)
Async XLA Ops:
  7.2 79.0 %all-gather.7.cloned.1.call-start = ((), (), s32[]{:S(2)}) async-start(), calls=%async_computation.1 | async-start | bytes 3276800 | tf_op jit(solution)/shard_map/all_gather | solution.py:21
  8.7 12.8 %collective-permute-start = (bf16[3,1536]{1,0:T(4,128)(2,1)S(1)}, bf16[3,1536]{1,0:T(4,128)(2,1)S(1)}, u32[]{:S(2)}, u32[]{:S(2)}) collective-permute-start(bf16[3,1536]{1,0:T(4,128)(2,1)S(1)} %pad_maximum_fusion.2), channel_id=1, source_target_pairs={{0,4},{4,8},{8,12},{1,5},{5,9},{9,13},{2,6},{6,10},{10,14},{3,7},{... | collective-permute-start | bytes 27656 | tf_op jit(solution)/shard_map/ppermute | solution.py:16
  15.3 6.1 %copy-start.4 = (f32[3,8,2,128]{3,1,2,0:T(8,128)}, f32[3,8,2,128]{3,1,2,0:T(8,128)S(1)}, u32[]{:S(2)}) copy-start(f32[3,8,2,128]{3,1,2,0:T(8,128)S(1)} %copy.45) | copy-start | bytes 73732
  16.3 5.1 %copy-start.5 = (f32[3,8,2,128]{3,1,2,0:T(8,128)}, f32[3,8,2,128]{3,1,2,0:T(8,128)S(1)}, u32[]{:S(2)}) copy-start(f32[3,8,2,128]{3,1,2,0:T(8,128)S(1)} %copy.46) | copy-start | bytes 73732
  31.0 115.7 %all-gather.5.cloned.1.call-start = ((), (), s32[]{:S(2)}) async-start(), calls=%async_computation | async-start | bytes 1638400 | tf_op jit(solution)/shard_map/all_gather | solution.py:151
  46.5 3.7 %copy-start.6 = (f32[3,8,2,128]{3,1,2,0:T(8,128)S(1)}, f32[3,8,2,128]{3,1,2,0:T(8,128)}, u32[]{:S(2)}) copy-start(f32[3,8,2,128]{3,1,2,0:T(8,128)} %copy-done.5) | copy-start | bytes 73732
  46.5 3.7 %copy-start.11 = (f32[20,256]{1,0:T(8,128)S(1)}, f32[20,256]{1,0:T(8,128)}, u32[]{:S(2)}) copy-start(f32[20,256]{1,0:T(8,128)} %get-tuple-element.73) | copy-start | bytes 61444
  86.3 0.7 copy-start.9
  86.3 1.3 copy-start.3
  87.6 4.2 %copy-start.13 = (f32[20]{0:T(128)S(1)}, f32[20]{0:T(128)}, u32[]{:S(2)}) copy-start(f32[20]{0:T(128)} %get-tuple-element.84) | copy-start | bytes 244
  89.0 3.2 %copy-start.8 = (f32[256,20]{0,1:T(8,128)S(1)}, f32[256,20]{0,1:T(8,128)}, u32[]{:S(2)}) copy-start(f32[256,20]{0,1:T(8,128)} %get-tuple-element.76) | copy-start | bytes 61444
  91.8 1.3 copy-start.2
  94.6 2.9 %copy-start.1 = (f32[256,1280]{1,0:T(8,128)S(1)}, f32[256,1280]{1,0:T(8,128)}, u32[]{:S(2)}) copy-start(f32[256,1280]{1,0:T(8,128)} %copy.40) | copy-start | bytes 3932164
  94.6 2.9 %copy-start.10 = (f32[1280]{0:T(1024)S(1)}, f32[1280]{0:T(1024)}, u32[]{:S(2)}) copy-start(f32[1280]{0:T(1024)} %mul.320) | copy-start | bytes 15364
  97.5 10.6 %copy-start.12 = (f32[1280]{0:T(1024)S(1)}, f32[1280]{0:T(1024)}, u32[]{:S(2)}) copy-start(f32[1280]{0:T(1024)} %param.23) | copy-start | bytes 15364
  110.1 38.2 %copy-start = (bf16[512,1280]{1,0:T(8,128)(2,1)}, bf16[512,1280]{1,0:T(8,128)(2,1)S(1)}, u32[]{:S(2)}) copy-start(bf16[512,1280]{1,0:T(8,128)(2,1)S(1)} %multiply_convert_fusion.4) | copy-start | bytes 3932164
  110.2 1.8 %copy-start.7 = (bf16[40,1280]{1,0:T(8,128)(2,1)S(1)}, bf16[40,1280]{1,0:T(8,128)(2,1)}, u32[]{:S(2)}) copy-start(bf16[40,1280]{1,0:T(8,128)(2,1)} %param.25) | copy-start | bytes 307204
  110.2 2.0 %copy-start.14 = (s32[40]{0:T(128)S(1)}, s32[40]{0:T(128)}, u32[]{:S(2)}) copy-start(s32[40]{0:T(128)} %param.27) | copy-start | bytes 484
  110.2 2.0 %copy-start.15 = (s32[40]{0:T(128)S(1)}, s32[40]{0:T(128)}, u32[]{:S(2)}) copy-start(s32[40]{0:T(128)} %param.26) | copy-start | bytes 484
Sparse Core Ops, SparseCore 0:
  31.1 55.0 all-gather.6
  112.1 34.5 all-gather.4
where the time goes:
time: 158 us; the launch traced here: 157 us
  waiting for transfers between devices  67.5 us (43%)
  other arithmetic  20 us (13%)
  local copies, waits for them, and re-layouts  18.7 us (12%)
  blocking collectives  16.5 us (10%)
  between operations  15.1 us (10%)
  matrix products  14.5 us (9%)
  starting transfers between devices  5.04 us (3%)
    all_gather x1, waiting for transfers between devices, local(): piece = lax.all_gather(summaries, 'seq', axis=0, tiled=True)  34.4 us
    all_gather x1, waiting for transfers between devices, prefix(): gathered = jax.tree.map(lambda a: lax.all_gather(a, axis), part)  33 us
    unnamed x1, blocking collectives  10.1 us
    dot_general x2, matrix products, stretch_local(): jnp.einsum('hij,jhp->ihp', mixing, x_block, preferred_element_type=jnp.fl...  6.59 us
    psum x1, blocking collectives, local(): square_sum = lax.psum(jnp.sum(gated * gated, axis=1), 'tensor')  6.37 us
    convert_element_type x2, other arithmetic, causal_conv(): return silu_act(summed).astype(jnp.bfloat16)  5.91 us
    concatenate x2, local copies, waits for them, and re-layouts, local(): jnp.concatenate(pieces_out, axis=0)  5.7 us
    ppermute x1, starting transfers between devices, passed_along(): lax.ppermute(value, axis, [(source, source + steps) for source in range(l...  4.96 us
  transfers between devices with their start and end apart: 3, of which 2 were waited for; matrix products, arithmetic and copies ran while one was open for 12% of the time, Pallas kernels for 0%

commit v1 on v0

--- a/solution.py
+++ b/solution.py
@@ -8,6 +8,19 @@
 POOL_HEADS = 32
 EPSILON = 1e-05
 MASKED = -1e30
+
+
+def ring_gather(array, axis, dim):
+    ways = lax.axis_size(axis)
+    up = [(d, (d + 1) % ways) for d in range(ways)]
+    down = [(d, (d - 1) % ways) for d in range(ways)]
+    earlier, later = ([array], [array])
+    for _ in range(ways // 2):
+        earlier.append(lax.ppermute(earlier[-1], axis, up))
+    for _ in range((ways - 1) // 2):
+        later.append(lax.ppermute(later[-1], axis, down))
+    line = jnp.concatenate([*earlier[::-1], *later[1:]], axis=dim)
+    return jnp.roll(line, (lax.axis_index(axis) - ways // 2) * array.shape[dim], axis=dim)
 
 
 def passed_along(value, axis, steps):
@@ -148,7 +161,7 @@
     scale_factor = 1.0 / math.sqrt(pool_width)
     pools_local = pool_query.shape[0]
     queries = pool_query.reshape(pools_local, pool_heads_local, pool_width)
-    piece = lax.all_gather(summaries, "seq", axis=0, tiled=True)
+    piece = ring_gather(summaries, "seq", 0)
     peak = jnp.full((pool_heads_local, pools_local), MASKED, jnp.float32)
     numer = jnp.zeros((pools_local, pool_heads_local, pool_width), jnp.float32)
     count = piece.shape[0]

time: 158 us -> 149 us (0.943)
  waiting for transfers between devices: 67.5 us -> 54.8 us
  starting transfers between devices: 5.04 us -> 9.58 us
    all_gather x1 -> x0, waiting for transfers between devices: 34.4 us -> none  [local(): piece = lax.all_gather(summaries, 'seq', axis=0, tiled=True)]
    ppermute x0 -> x3, waiting for transfers between devices: none -> 21.7 us  [the longest x2 19.3 us: ring_gather(): earlier.append(lax.ppermute(earlier[-1], axis, up))]
    ppermute x0 -> x3, starting transfers between devices: none -> 4.59 us  [the longest x1 3.87 us: ring_gather(): later.append(lax.ppermute(later[-1], axis, down))]
    all_gather x1 -> x0, local copies, waits for them, and re-layouts: 1.6 us -> none  [local(): piece = lax.all_gather(summaries, 'seq', axis=0, tiled=True)]
    unnamed x39 -> x44, local copies, waits for them, and re-layouts: 4.11 us -> 4.22 us
  transfers between devices with their start and end apart: 3 -> 5, of which waited for: 2 -> 4; matrix products, arithmetic and copies ran while one was open for 12% -> 13% of each run, Pallas kernels for 0% -> 0%
where the time goes in v1:
time: 149 us; the launch traced here: 148 us
  waiting for transfers between devices  54.8 us (37%)
  other arithmetic  19.5 us (13%)
  local copies, waits for them, and re-layouts  18 us (12%)
  blocking collectives  16.5 us (11%)
  between operations  15.2 us (10%)
  matrix products  14.5 us (10%)
  starting transfers between devices  9.58 us (6%)
    all_gather x1, waiting for transfers between devices, prefix(): gathered = jax.tree.map(lambda a: lax.all_gather(a, axis), part)  33.1 us
    ppermute x2, waiting for transfers between devices, ring_gather(): earlier.append(lax.ppermute(earlier[-1], axis, up))  19.3 us
    unnamed x1, blocking collectives  10.1 us
    dot_general x2, matrix products, stretch_local(): jnp.einsum('hij,jhp->ihp', mixing, x_block, preferred_element_type=jnp.fl...  6.59 us
    psum x1, blocking collectives, local(): square_sum = lax.psum(jnp.sum(gated * gated, axis=1), 'tensor')  6.37 us
    convert_element_type x2, other arithmetic, causal_conv(): return silu_act(summed).astype(jnp.bfloat16)  5.91 us
    concatenate x2, local copies, waits for them, and re-layouts, local(): jnp.concatenate(pieces_out, axis=0)  5.7 us
    ppermute x1, starting transfers between devices, passed_along(): lax.ppermute(value, axis, [(source, source + steps) for source in range(l...  4.96 us
  transfers between devices with their start and end apart: 5, of which 4 were waited for; matrix products, arithmetic and copies ran while one was open for 13% of the time, Pallas kernels for 0%

profile of v1, /device:TPU:0, one launch (start us, length us, event | category | flops | bytes accessed | tf_op | source)
XLA Modules:
  0.0 148.1 jit_solution(9848683213221025026)
XLA Ops:
  7.2 0.7 slice.120
  7.9 0.7 slice.121
  8.7 5.0 %collective-permute-start = (bf16[3,1536]{1,0:T(4,128)(2,1)S(1)}, bf16[3,1536]{1,0:T(4,128)(2,1)S(1)}, u32[]{:S(2)}, u32[]{:S(2)}) collective-permute-start(bf16[3,1536]{1,0:T(4,128)(2,1)S(1)} %pad_maximum_fusion.2), channel_id=1, source_target_pairs={{0,4},{4,8},{8,12},{1,5},{5,9},{9,13},{2,6},{6,10},{10,14},{3,7},{... | collective-permute-start | bytes 27656 | tf_op jit(solution)/shard_map/ppermute | solution.py:29
  13.6 0.8 fusion.71
  14.4 0.6 reduce-window.14
  15.0 0.2 slice_reduce_fusion.1
  15.4 0.6 reduce-window.16
  16.0 0.2 slice_reduce_fusion
  16.2 0.1 broadcast_add_fusion
  16.3 0.8 slice_convert_fusion.3
  17.2 0.8 slice_reduce_fusion.2
  17.9 0.5 fusion.72
  18.5 1.5 fusion.70
  19.9 0.9 convert_reduce_fusion.3
  20.8 0.6 exp.65
  21.5 4.0 %divide_convert_fusion = bf16[512,1280]{1,0:T(8,128)(2,1)S(1)} fusion(bf16[512,1280]{1,0:T(8,128)(2,1)} %param.15, bf16[3,1280]{1,0:T(4,128)(2,1)S(1)} %slice.158, f32[1280]{0:T(1024)S(1)} %get-tuple-element.52, f32[1280]{0:T(1024)S(1)} %get-tuple-element.53, f32[1280]{0:T(1024)S(1)} %get-tuple-element.51, f32[1280]{0:T(1024)S(1)} %get-tuple-element.50), kind=kLoop, calls=%fused_computation.25 | loop fusion | flops 15728640 | bytes 2649600 | tf_op jit(solution)/shard_map/convert_element_type | solution.py:58
  25.5 0.1 fusion.69
  25.6 0.2 copy.34
  25.8 0.2 copy.39
  26.1 1.9 %divide_convert_fusion.1 = bf16[512,256]{1,0:T(8,128)(2,1)S(1)} fusion(bf16[512,256]{1,0:T(8,128)(2,1)} %param.17, bf16[3,256]{1,0:T(4,128)(2,1)S(1)} %slice.165, f32[256]{0:T(256)S(1)} %bitcast.90, f32[256]{0:T(256)S(1)} %bitcast.91, f32[256]{0:T(256)S(1)} %bitcast.89, f32[256]{0:T(256)S(1)} %bitcast.88), kind=kLoop, calls=%fused_computation.59 | loop fusion | flops 3145728 | bytes 529920 | tf_op jit(solution)/shard_map/convert_element_type | solution.py:58
  28.0 1.1 convolution_add_fusion.3
  29.1 1.9 %convolution_add_fusion.2 = f32[20,64,128]{2,1,0:T(8,128)} fusion(bf16[256,20,64]{0,2,1:T(8,128)(2,1)S(1)} %bitcast.75, f32[256,20]{0,1:T(8,128)} %get-tuple-element.72, f32[20,64,128]{2,1,0:T(8,128)S(1)} %convolution_add_fusion.3, f32[20]{0:T(128)} %exp.65, bf16[512,256]{1,0:T(8,128)(2,1)S(1)} %divide_convert_fusion.1), kind=kOutput, calls=%fused_computation.43 | convolution fusion | flops 85196800 | bytes 2052176 | tf_op jit(solution)/shard_map/jhp,js->hps/dot_general | solution.py:74
  31.0 1.2 dynamic-slice
  32.9 0.9 dynamic-update-slice
  33.8 10.1 %all-reduce = f32[80]{0:T(128)S(1)} all-reduce(f32[80]{0:T(128)S(1)} %dynamic-update-slice), channel_id=2, replica_groups=mesh['groups'=2,'seq'=4,'tensor'=4] {'seq'}, use_global_device_ids=true, to_apply=%add | all-reduce | flops 80 | bytes 640
  43.9 0.1 reshape.210
  44.0 0.7 mul.322
  44.7 0.7 mul.323
  45.4 0.7 compare_and_fusion
  46.1 0.2 fusion.57
  46.3 0.2 fusion.53
  46.5 3.7 %fusion.18 = f32[256,20,64]{0,2,1:T(8,128)} fusion(bf16[256,20,64]{0,2,1:T(8,128)(2,1)S(1)} %bitcast.78, f32[20,256]{1,0:T(8,128)} %get-tuple-element.70, f32[256,256]{1,0:T(8,128)S(1)} %fusion.57, f32[20,256]{1,0:T(8,128)} %bitcast.81, pred[256,256]{1,0:T(8,128)(4,1)S(1)} %iota_compare_fusion), kind=kOutput, calls=%fused_computation.31 | convolution fusion | flops 175636480 | bytes 2334720 | tf_op jit(solution)/shard_map/hij,jhp->ihp/dot_general | solution.py:71
  50.2 2.9 %fusion.17 = f32[256,20,64]{0,2,1:T(8,128)} fusion(bf16[256,20,64]{0,2,1:T(8,128)(2,1)S(1)} %bitcast.76, f32[20,256]{1,0:T(8,128)S(1)} %copy-done.11, f32[256,256]{1,0:T(8,128)S(1)} %fusion.53, f32[20,256]{1,0:T(8,128)S(1)} %bitcast.84, pred[256,256]{1,0:T(8,128)(4,1)S(1)} %iota_compare_fusion), kind=kOutput, calls=%fused_computation.30 | convolution fusion | flops 175636480 | bytes 2334720 | tf_op jit(solution)/shard_map/hij,jhp->ihp/dot_general | solution.py:71
  53.1 33.1 %all-gather.4.cloned.1.call-done = f32[80,64,128]{2,1,0:T(8,128)} async-done(((f32[20,64,128]{2,1,0:T(8,128)}), f32[80,64,128]{2,1,0:T(8,128)}) %all-gather.4.cloned.1.call-update) | async-done | bytes 2621456 | tf_op jit(solution)/shard_map/all_gather | solution.py:34
  86.3 0.3 fusion.44
  86.6 0.4 copy-done.9
  87.0 0.6 copy-done.3
  87.6 1.4 fusion.21
  89.0 2.8 %copy.40 = f32[256,1280]{1,0:T(8,128)} copy(f32[256,1280]{0,1:T(8,128)} %bitcast.73) | data formatting | bytes 2621440 | tf_op jit(solution)/shard_map/concatenate | solution.py:148
  91.8 0.4 fusion.41
  92.2 0.9 copy-done.2
  93.1 1.4 fusion.22
  94.6 2.9 %copy.41 = f32[256,1280]{1,0:T(8,128)} copy(f32[256,1280]{0,1:T(8,128)} %bitcast.72) | data formatting | bytes 2621440 | tf_op jit(solution)/shard_map/concatenate | solution.py:148
  97.5 4.2 %multiply_reduce_fusion = (f32[512]{0:T(512)S(1)}, f32[512,1280]{1,0:T(8,128)}) fusion(bf16[512,1280]{1,0:T(8,128)(2,1)} %param.16, bf16[512,1280]{1,0:T(8,128)(2,1)S(1)} %divide_convert_fusion, f32[1280]{0:T(1024)S(1)} %copy-done.10, f32[256,1280]{1,0:T(8,128)} %copy.41, f32[256,1280]{1,0:T(8,128)S(1)} %copy-done.1), kind=kLoop, calls=%fused_computation.14 | loop fusion | flops 7208448 | bytes 7871488 | tf_op jit(solution)/shard_map/reduce_sum | solution.py:152
  101.7 6.4 %psum.7 = f32[512]{0:T(512)S(1)} all-reduce(f32[512]{0:T(512)S(1)} %get-tuple-element.66), channel_id=1, replica_groups=mesh['groups'=2,'seq'=4,'tensor'=4] {'tensor'}, use_global_device_ids=true, to_apply=%region_7.8 | all-reduce | flops 512 | bytes 4096 | tf_op jit(solution)/shard_map/psum | solution.py:152
  108.1 2.0 %multiply_convert_fusion.4 = bf16[512,1280]{1,0:T(8,128)(2,1)S(1)} fusion(f32[512,1280]{1,0:T(8,128)} %get-tuple-element.67, f32[1280]{0:T(1024)S(1)} %copy-done.12, f32[512]{0:T(512)S(1)} %add_rsqrt_fusion), kind=kLoop, calls=%fused_computation.13 | loop fusion | flops 1966080 | bytes 3939328 | tf_op jit(solution)/shard_map/convert_element_type | solution.py:156
  110.2 0.9 gather_fusion
  111.1 0.1 broadcast_select_fusion
  111.2 0.7 collective-permute-start.1
  111.9 11.1 %collective-permute-done.1 = bf16[128,1280]{1,0:T(8,128)(2,1)S(1)} collective-permute-done((bf16[128,1280]{1,0:T(8,128)(2,1)S(1)}, bf16[128,1280]{1,0:T(8,128)(2,1)S(1)}, u32[]{:S(2)}, u32[]{:S(2)}) %collective-permute-start.1) | collective-permute-done | bytes 327712 | tf_op jit(solution)/shard_map/ppermute | solution.py:19
  123.0 0.2 reshape.192
  123.3 0.1 fusion.46
  123.3 3.9 %collective-permute-start.3 = (bf16[128,1280]{1,0:T(8,128)(2,1)S(1)}, bf16[128,1280]{1,0:T(8,128)(2,1)S(1)}, u32[]{:S(2)}, u32[]{:S(2)}) collective-permute-start(bf16[128,1280]{1,0:T(8,128)(2,1)S(1)} %broadcast_select_fusion), channel_id=1, source_target_pairs={{0,12},{4,0},{8,4},{12,8},{1,13},{5,1},{9,5},{13,9},{2,14},{6,2},{... | collective-permute-start | bytes 983048 | tf_op jit(solution)/shard_map/ppermute | solution.py:21
  127.2 8.2 %collective-permute-done.2 = bf16[128,1280]{1,0:T(8,128)(2,1)S(1)} collective-permute-done((bf16[128,1280]{1,0:T(8,128)(2,1)S(1)}, bf16[128,1280]{1,0:T(8,128)(2,1)S(1)}, u32[]{:S(2)}, u32[]{:S(2)}) %collective-permute-start.2) | collective-permute-done | bytes 327712 | tf_op jit(solution)/shard_map/ppermute | solution.py:19
  135.4 0.1 constant_dynamic-update-slice_fusion.5
  135.6 2.4 %collective-permute-done.3 = bf16[128,1280]{1,0:T(8,128)(2,1)S(1)} collective-permute-done((bf16[128,1280]{1,0:T(8,128)(2,1)S(1)}, bf16[128,1280]{1,0:T(8,128)(2,1)S(1)}, u32[]{:S(2)}, u32[]{:S(2)}) %collective-permute-start.3) | collective-permute-done | bytes 327712 | tf_op jit(solution)/shard_map/ppermute | solution.py:21
  138.1 0.1 constant_dynamic-update-slice_fusion.1
  138.3 0.1 constant_dynamic-slice_fusion
  138.4 0.7 copy.42
  139.0 0.4 fusion.73
  139.5 0.3 fusion.31
  139.7 0.6 fusion.28
  140.3 0.1 copy.44
  140.4 0.8 reshape.193
  (64 shorter events, 0.7 us)
Async XLA Ops:
  7.2 79.0 %all-gather.4.cloned.1.call-start = ((), (), s32[]{:S(2)}) async-start(), calls=%async_computation | async-start | bytes 3276800 | tf_op jit(solution)/shard_map/all_gather | solution.py:34
  8.7 12.8 %collective-permute-start = (bf16[3,1536]{1,0:T(4,128)(2,1)S(1)}, bf16[3,1536]{1,0:T(4,128)(2,1)S(1)}, u32[]{:S(2)}, u32[]{:S(2)}) collective-permute-start(bf16[3,1536]{1,0:T(4,128)(2,1)S(1)} %pad_maximum_fusion.2), channel_id=1, source_target_pairs={{0,4},{4,8},{8,12},{1,5},{5,9},{9,13},{2,6},{6,10},{10,14},{3,7},{... | collective-permute-start | bytes 27656 | tf_op jit(solution)/shard_map/ppermute | solution.py:29
  15.3 6.1 %copy-start.4 = (f32[3,8,2,128]{3,1,2,0:T(8,128)}, f32[3,8,2,128]{3,1,2,0:T(8,128)S(1)}, u32[]{:S(2)}) copy-start(f32[3,8,2,128]{3,1,2,0:T(8,128)S(1)} %copy.45) | copy-start | bytes 73732
  16.3 5.1 %copy-start.5 = (f32[3,8,2,128]{3,1,2,0:T(8,128)}, f32[3,8,2,128]{3,1,2,0:T(8,128)S(1)}, u32[]{:S(2)}) copy-start(f32[3,8,2,128]{3,1,2,0:T(8,128)S(1)} %copy.46) | copy-start | bytes 73732
  46.5 3.7 %copy-start.6 = (f32[3,8,2,128]{3,1,2,0:T(8,128)S(1)}, f32[3,8,2,128]{3,1,2,0:T(8,128)}, u32[]{:S(2)}) copy-start(f32[3,8,2,128]{3,1,2,0:T(8,128)} %copy-done.5) | copy-start | bytes 73732
  46.5 3.7 %copy-start.11 = (f32[20,256]{1,0:T(8,128)S(1)}, f32[20,256]{1,0:T(8,128)}, u32[]{:S(2)}) copy-start(f32[20,256]{1,0:T(8,128)} %get-tuple-element.73) | copy-start | bytes 61444
  86.3 0.7 copy-start.9
  86.3 1.3 copy-start.3
  87.6 4.2 %copy-start.13 = (f32[20]{0:T(128)S(1)}, f32[20]{0:T(128)}, u32[]{:S(2)}) copy-start(f32[20]{0:T(128)} %get-tuple-element.84) | copy-start | bytes 244
  89.0 3.2 %copy-start.8 = (f32[256,20]{0,1:T(8,128)S(1)}, f32[256,20]{0,1:T(8,128)}, u32[]{:S(2)}) copy-start(f32[256,20]{0,1:T(8,128)} %get-tuple-element.76) | copy-start | bytes 61444
  91.8 1.3 copy-start.2
  94.6 2.9 %copy-start.1 = (f32[256,1280]{1,0:T(8,128)S(1)}, f32[256,1280]{1,0:T(8,128)}, u32[]{:S(2)}) copy-start(f32[256,1280]{1,0:T(8,128)} %copy.40) | copy-start | bytes 3932164
  94.6 2.9 %copy-start.10 = (f32[1280]{0:T(1024)S(1)}, f32[1280]{0:T(1024)}, u32[]{:S(2)}) copy-start(f32[1280]{0:T(1024)} %mul.323) | copy-start | bytes 15364
  97.5 10.6 %copy-start.12 = (f32[1280]{0:T(1024)S(1)}, f32[1280]{0:T(1024)}, u32[]{:S(2)}) copy-start(f32[1280]{0:T(1024)} %param.23) | copy-start | bytes 15364
  110.1 25.4 %copy-start = (bf16[512,1280]{1,0:T(8,128)(2,1)}, bf16[512,1280]{1,0:T(8,128)(2,1)S(1)}, u32[]{:S(2)}) copy-start(bf16[512,1280]{1,0:T(8,128)(2,1)S(1)} %multiply_convert_fusion.4) | copy-start | bytes 3932164
  110.2 12.9 %copy-start.7 = (bf16[40,1280]{1,0:T(8,128)(2,1)S(1)}, bf16[40,1280]{1,0:T(8,128)(2,1)}, u32[]{:S(2)}) copy-start(bf16[40,1280]{1,0:T(8,128)(2,1)} %param.25) | copy-start | bytes 307204
  110.2 13.1 %copy-start.14 = (s32[40]{0:T(128)S(1)}, s32[40]{0:T(128)}, u32[]{:S(2)}) copy-start(s32[40]{0:T(128)} %param.27) | copy-start | bytes 484
  110.2 13.1 %copy-start.15 = (s32[40]{0:T(128)S(1)}, s32[40]{0:T(128)}, u32[]{:S(2)}) copy-start(s32[40]{0:T(128)} %param.26) | copy-start | bytes 484
  111.2 11.8 %collective-permute-start.1 = (bf16[128,1280]{1,0:T(8,128)(2,1)S(1)}, bf16[128,1280]{1,0:T(8,128)(2,1)S(1)}, u32[]{:S(2)}, u32[]{:S(2)}) collective-permute-start(bf16[128,1280]{1,0:T(8,128)(2,1)S(1)} %broadcast_select_fusion), channel_id=1, source_target_pairs={{0,4},{4,8},{8,12},{12,0},{1,5},{5,9},{9,13},{13,1},{2,6},{6,10},{... | collective-permute-start | bytes 983048 | tf_op jit(solution)/shard_map/ppermute | solution.py:19
  123.0 12.4 %collective-permute-start.2 = (bf16[128,1280]{1,0:T(8,128)(2,1)S(1)}, bf16[128,1280]{1,0:T(8,128)(2,1)S(1)}, u32[]{:S(2)}, u32[]{:S(2)}) collective-permute-start(bf16[128,1280]{1,0:T(8,128)(2,1)S(1)} %collective-permute-done.1), channel_id=1, source_target_pairs={{0,4},{4,8},{8,12},{12,0},{1,5},{5,9},{9,13},{13,1},{2,6},{6,10},{... | collective-permute-start | bytes 983048 | tf_op jit(solution)/shard_map/ppermute | solution.py:19
  123.3 14.7 %collective-permute-start.3 = (bf16[128,1280]{1,0:T(8,128)(2,1)S(1)}, bf16[128,1280]{1,0:T(8,128)(2,1)S(1)}, u32[]{:S(2)}, u32[]{:S(2)}) collective-permute-start(bf16[128,1280]{1,0:T(8,128)(2,1)S(1)} %broadcast_select_fusion), channel_id=1, source_target_pairs={{0,12},{4,0},{8,4},{12,8},{1,13},{5,1},{9,5},{13,9},{2,14},{6,2},{... | collective-permute-start | bytes 983048 | tf_op jit(solution)/shard_map/ppermute | solution.py:21
Sparse Core Ops, SparseCore 0:
  31.1 55.0 all-gather.3
